TPU v7x, 256 devices: a whole 4x4x8 slice. The times are simulated.
256 devices in a mesh: gx: 16 (over z, core), gy: 16 (over x, y).
Axes of the slice: x: 4, y: 4, z: 8, core: 2. Of those that a mesh axis runs over, the one named last changes fastest.
Arguments:
- state: bfloat16 [2, 256, 768, 2048], P(None, None, 'gx', 'gy'), as said below
Outputs:
- modes: bfloat16 [255, 2, 768, 2048], P(None, None, 'gx', 'gy')
- reduced: float32 [255, 255], replicated
Inputs may be any that keep to these rules, and one draw needn't show every extreme that they name: `state`: both fields are positive.
All inputs are finite; a program needn't handle non-finite values.
Results may differ from a plain program's by a relative error of at most 0.0077.
Values may be sent and summed in bfloat16 or wider, within the bound.
No kernel may reach another device: no remote copies, remote signals or barrier semaphores. Data moves between devices by JAX's collectives and lax.ppermute only.
A program may use at most 128 MiB of HBM per device.

v0:
```python
import jax
import jax.numpy as jnp
from jax import lax
from jax.sharding import PartitionSpec as P


def padded_2(cells, sides, width):
    for axis, dim in sides:
        count = lax.axis_size(axis)
        ends = count - 1
        head = lax.slice_in_dim(cells, 0, width, axis=dim)
        tail = lax.slice_in_dim(cells, cells.shape[dim] - width, cells.shape[dim], axis=dim)
        cells = jnp.concatenate(
            [
                lax.ppermute(tail, axis, [(i, (i + 1) % count) for i in range(ends)]),
                cells,
                lax.ppermute(head, axis, [((i + 1) % count, i) for i in range(ends)]),
            ],
            axis=dim,
        )
    return cells


def tri_solve(lower, right):
    return lax.linalg.triangular_solve(lower, right, left_side=True, lower=True)


def gradients(padded):
    grad_x = (
        padded[:, :-4, 2:-2]
        - 8.0 * padded[:, 1:-3, 2:-2]
        + 8.0 * padded[:, 3:-1, 2:-2]
        - padded[:, 4:, 2:-2]
    ) / 12.0
    grad_y = (
        padded[:, 2:-2, :-4]
        - 8.0 * padded[:, 2:-2, 1:-3]
        + 8.0 * padded[:, 2:-2, 3:-1]
        - padded[:, 2:-2, 4:]
    ) / 12.0
    return jnp.stack([grad_x, grad_y], axis=1).astype(jnp.bfloat16)


def shards(state):
    snaps = state.shape[1]
    rows_x = state.shape[2]
    rows_y = state.shape[3]
    total_rows = 2 * rows_x * rows_y * lax.axis_size("gx") * lax.axis_size("gy")
    temp = 0.4 * state[1].astype(jnp.float32) / state[0].astype(jnp.float32)
    padded = padded_2(temp, (("gx", 1), ("gy", 2)), 2)
    features = gradients(padded)
    snap = features.reshape(snaps, 2 * rows_x * rows_y)
    local_gram = (
        lax.dot_general(snap, snap, (((1,), (1,)), ((), ())), preferred_element_type=jnp.float32)
        / total_rows
    )
    gram = lax.psum(local_gram, ("gx", "gy"))
    lower = jnp.linalg.cholesky(gram[: snaps - 1, : snaps - 1])
    cross = gram[: snaps - 1, 1:]
    half = tri_solve(lower, cross)
    reduced = tri_solve(lower, half.T).T
    inverse = tri_solve(lower, jnp.eye(snaps - 1, dtype=jnp.float32)).astype(jnp.bfloat16)
    modes = jnp.dot(inverse, snap[1:], preferred_element_type=jnp.float32).astype(jnp.bfloat16)
    return (modes.reshape(snaps - 1, 2, rows_x, rows_y), reduced)


def solution(mesh):
    placed = (P(None, None, "gx", "gy"),)
    return jax.shard_map(
        shards,
        mesh=mesh,
        in_specs=placed,
        out_specs=(P(None, None, "gx", "gy"), P()),
        check_vma=False,
    )
```

profile of v0, /device:TPU:2, one launch (start us, length us, event | category | flops | bytes accessed | tf_op | source)
XLA Modules:
  0.0 435.9 jit_solution(15575594914575890213)
XLA Ops:
  7.2 3.9 fusion.44
  12.5 1.8 collective-permute-start
  16.3 3.1 collective-permute-done.1
  20.1 3.6 pad_maximum_fusion.1
  23.7 11.6 %fusion.42 = (f32[256,52,2]{2,0,1:T(8,128)}, f32[256,52,2]{2,0,1:T(8,128)}) fusion(f32[256,52,128]{2,0,1:T(8,128)} %pad_maximum_fusion.1), kind=kLoop, calls=%fused_computation.88 | loop fusion | bytes 425984 | tf_op jit(solution)/shard_map/slice | solution.py:12
  35.4 4.7 %copy.16 = f32[256,52,2]{0,2,1:T(2,128)S(1)} copy(f32[256,52,2]{2,0,1:T(8,128)} %get-tuple-element.41) | data formatting | bytes 212992 | tf_op jit(solution)/shard_map/slice | solution.py:12
  40.1 3.5 collective-permute-start.2
  43.6 5.3 %copy.18 = f32[256,52,2]{0,2,1:T(2,128)} copy(f32[256,52,2]{2,0,1:T(8,128)} %get-tuple-element.42) | data formatting | bytes 212992 | tf_op jit(solution)/shard_map/slice | solution.py:11
  48.9 4.6 %collective-permute-start.3 = (f32[256,52,2]{0,2,1:T(2,128)}, f32[256,52,2]{0,2,1:T(2,128)}, u32[]{:S(2)}, u32[]{:S(2)}) collective-permute-start(f32[256,52,2]{0,2,1:T(2,128)} %copy.18), channel_id=1, source_target_pairs={{1,0},{2,1},{3,2},{4,3},{5,4},{6,5},{7,6},{8,7},{9,8},{10,9},{11,1... | collective-permute-start | bytes 319496 | tf_op jit(solution)/shard_map/ppermute | solution.py:17
  53.5 11.1 %fusion.17 = bf16[256,1,48,128]{3,0,2,1:T(8,128)(2,1)S(1)} fusion(f32[256,2,128]{2,0,1:T(8,128)} %copy-done.2, f32[256,48,128]{2,0,1:T(8,128)} %copy-done, f32[256,2,128]{2,0,1:T(8,128)S(1)} %collective-permute-done), kind=kLoop, calls=%fused_computation.36 | loop fusion | flops 17301504 | bytes 9961472 | tf_op jit(solution)/shard_map/stack | solution.py:41
  64.6 5.0 %copy.17 = f32[256,52,2]{2,0,1:T(8,128)} copy(f32[256,52,2]{0,2,1:T(2,128)} %collective-permute-done.2) | data formatting | bytes 212992 | tf_op jit(solution)/shard_map/ppermute | solution.py:15
  69.6 5.1 %copy.19 = f32[256,52,2]{2,0,1:T(8,128)} copy(f32[256,52,2]{0,2,1:T(2,128)} %collective-permute-done.3) | data formatting | bytes 212992 | tf_op jit(solution)/shard_map/ppermute | solution.py:17
  74.7 21.0 %fusion.18 = bf16[256,1,48,128]{3,0,2,1:T(8,128)(2,1)S(1)} fusion(f32[256,52,2]{2,0,1:T(8,128)} %copy.19, f32[256,2,128]{2,0,1:T(8,128)} %copy-done.2, f32[256,48,128]{2,0,1:T(8,128)} %copy-done, f32[256,2,128]{2,0,1:T(8,128)S(1)} %collective-permute-done, f32[256,52,2]{2,0,1:T(8,128)} %copy.17), kind=kLoop, calls=%fused_computation.37 | loop fusion | flops 29884416 | bytes 10174464 | tf_op jit(solution)/shard_map/stack | solution.py:41
  95.8 1.7 copy-done.1
  97.4 2.5 fusion.20
  100.0 5.9 %fusion.8 = bf16[255,2,48,128]{3,0,2,1:T(8,128)(2,1)} fusion(bf16[256,1,48,128]{3,0,2,1:T(8,128)(2,1)S(1)} %fusion.17, bf16[256,1,48,128]{3,0,2,1:T(8,128)(2,1)} %copy-done.1), kind=kLoop, calls=%fused_computation.17 | loop fusion | flops 3133440 | bytes 12558336 | tf_op jit(solution)/shard_map/stack | solution.py:41
  105.8 8.7 %copy.22 = bf16[255,2,48,128]{0,3,2,1:T(8,128)(2,1)} copy(bf16[255,2,48,128]{3,0,2,1:T(8,128)(2,1)} %fusion.8) | data formatting | bytes 12533760 | tf_op jit(solution)/shard_map/slice | solution.py:63
  114.5 240.5 %all-reduce.4.cloned.1.call-done = f32[256,256]{0,1:T(8,128)} async-done(((f32[256,256]{0,1:T(8,128)}), f32[256,256]{0,1:T(8,128)}) %all-reduce.4.cloned.1.call-update) | async-done | bytes 262160 | tf_op jit(solution)/shard_map/psum | solution.py:57
  357.1 11.7 %cholesky.51 = f32[128,128]{1,0:T(8,128)S(1)} custom-call(f32[128,128]{1,0:T(8,128)S(1)} %cholesky.124), custom_call_target="Cholesky" | custom-call | tf_op jit(solution)/shard_map/jit(cholesky)/cholesky | solution.py:58
  368.9 9.8 %custom-call.14 = f32[1,128,128]{1,2,0:T(8,128)S(1)} custom-call(f32[1,128,128]{2,1,0:T(8,128)S(1)} %get-tuple-element.50), custom_call_target="InvertDiagBlocksLowerTriangular" | custom-call | tf_op jit(solution)/shard_map/jit(cholesky)/cholesky | solution.py:58
  379.2 11.6 %cholesky.110 = f32[127,127]{1,0:T(8,128)S(1)} custom-call(f32[127,127]{1,0:T(8,128)S(1)} %convolution_subtract_fusion.2), custom_call_target="Cholesky" | custom-call | tf_op jit(solution)/shard_map/jit(cholesky)/cholesky | solution.py:58
  393.6 19.9 %custom-call.17 = f32[2,128,128]{1,2,0:T(8,128)S(1)} custom-call(f32[2,128,128]{2,1,0:T(8,128)S(1)} %pad_maximum_fusion.15), custom_call_target="InvertDiagBlocksLowerTriangular" | custom-call | tf_op jit(solution)/shard_map/triangular_solve/custom-call.0 | solution.py:25
  419.2 4.6 %convolution_convert_fusion = bf16[255,12288]{1,0:T(8,128)(2,1)S(1)} fusion(bf16[255,12288]{0,1:T(8,128)(2,1)} %bitcast.61, bf16[127,255]{1,0:T(8,128)(2,1)S(1)} %fusion.35, f32[128,255]{1,0:T(8,128)S(1)} %fusion.28), kind=kOutput, calls=%fused_computation | convolution fusion | flops 1601447936 | bytes 12729090 | tf_op jit(solution)/shard_map/dot_general | solution.py:63
  425.3 3.8 slice.212
  (45 shorter events, 15.3 us)
Async XLA Ops:
  7.2 347.8 %all-reduce.4.cloned.1.call-start = ((), (), s32[]{:S(2)}) async-start(), calls=%async_computation | async-start | bytes 524288 | tf_op jit(solution)/shard_map/psum | solution.py:57
  12.5 6.9 %copy-start = (f32[256,48,128]{2,0,1:T(8,128)}, f32[256,48,128]{2,0,1:T(8,128)S(1)}, u32[]{:S(2)}) copy-start(f32[256,48,128]{2,0,1:T(8,128)S(1)} %divide_bitcast_fusion) | copy-start | bytes 18874372
  12.5 3.8 collective-permute-start
  14.3 5.1 %collective-permute-start.1 = (f32[256,2,128]{2,0,1:T(8,128)S(1)}, f32[256,2,128]{2,0,1:T(8,128)S(1)}, u32[]{:S(2)}, u32[]{:S(2)}) collective-permute-start(f32[256,2,128]{2,0,1:T(8,128)S(1)} %get-tuple-element.44), channel_id=1, source_target_pairs={{16,0},{32,16},{48,32},{64,48},{80,64},{96,80},{112,96},{128,112},... | collective-permute-start | bytes 786440 | tf_op jit(solution)/shard_map/ppermute | solution.py:17
  19.4 0.7 copy-start.2
  40.1 24.5 %collective-permute-start.2 = (f32[256,52,2]{0,2,1:T(2,128)S(1)}, f32[256,52,2]{0,2,1:T(2,128)}, u32[]{:S(2)}, u32[]{:S(2)}) collective-permute-start(f32[256,52,2]{0,2,1:T(2,128)S(1)} %copy.16), channel_id=1, source_target_pairs={{0,1},{1,2},{2,3},{3,4},{4,5},{5,6},{6,7},{7,8},{8,9},{9,10},{10,1... | collective-permute-start | bytes 319496 | tf_op jit(solution)/shard_map/ppermute | solution.py:15
  48.9 20.7 %collective-permute-start.3 = (f32[256,52,2]{0,2,1:T(2,128)}, f32[256,52,2]{0,2,1:T(2,128)}, u32[]{:S(2)}, u32[]{:S(2)}) collective-permute-start(f32[256,52,2]{0,2,1:T(2,128)} %copy.18), channel_id=1, source_target_pairs={{1,0},{2,1},{3,2},{4,3},{5,4},{6,5},{7,6},{8,7},{9,8},{10,9},{11,1... | collective-permute-start | bytes 319496 | tf_op jit(solution)/shard_map/ppermute | solution.py:17
  95.8 1.7 copy-start.1
  105.8 287.6 %copy-start.4 = (f32[128,1]{1,0:T(8,128)S(1)}, f32[128,1]{1,0:T(8,128)}, u32[]{:S(2)}) copy-start(f32[128,1]{1,0:T(8,128)} %constant.87.clone.3) | copy-start | bytes 1540
  114.5 303.8 %copy-start.3 = (f32[255,255]{1,0:T(8,128)S(1)}, f32[255,255]{1,0:T(8,128)}, u32[]{:S(2)}) copy-start(f32[255,255]{1,0:T(8,128)} %fusion.22) | copy-start | bytes 780304
Sparse Core Ops, SparseCore 0:
  100.1 254.8 all-reduce.3
where the time goes:
time: 437 us; the launch traced here: 436 us
  waiting for transfers between devices  244 us (56%)
  other arithmetic  99.2 us (23%)
  local copies, waits for them, and re-layouts  53.9 us (12%)
  between operations  15.6 us (4%)
  matrix products  12.3 us (3%)
  starting transfers between devices  11.2 us (3%)
    psum x1, waiting for transfers between devices, shards(): gram = lax.psum(local_gram, ('gx', 'gy'))  240 us
    another operation x3, other arithmetic, gradients(): return jnp.stack([grad_x, grad_y], axis=1).astype(jnp.bfloat16)  38 us
    another operation x7, other arithmetic, shards(): lower = jnp.linalg.cholesky(gram[:snaps - 1, :snaps - 1])  34.5 us
    another operation x4, other arithmetic, tri_solve(): return lax.linalg.triangular_solve(lower, right, left_side=True, lower=True)  20.1 us
    slice x3, local copies, waits for them, and re-layouts, padded_2(): lax.slice_in_dim(cells, cells.shape[dim] - width, cells.shape[dim], axis=...  16.4 us
  transfers between devices with their start and end apart: 5, of which 2 were waited for; matrix products, arithmetic and copies ran while one was open for 8% of the time, Pallas kernels for 0%

commit v1 on v0

--- a/solution.py
+++ b/solution.py
@@ -54,7 +54,9 @@
         lax.dot_general(snap, snap, (((1,), (1,)), ((), ())), preferred_element_type=jnp.float32)
         / total_rows
     )
-    gram = lax.psum(local_gram, ("gx", "gy"))
+    gram = local_gram
+    for over in ("gy", "gx"):
+        gram = lax.psum(gram, over)
     lower = jnp.linalg.cholesky(gram[: snaps - 1, : snaps - 1])
     cross = gram[: snaps - 1, 1:]
     half = tri_solve(lower, cross)

time: 437 us -> 392 us (0.90)
  waiting for transfers between devices: 244 us -> 198 us
    psum x1 -> x2, waiting for transfers between devices: 240 us -> 194 us  [shards(): gram = lax.psum(gram, over)]
  transfers between devices with their start and end apart: 5 -> 6, of which waited for: 2 -> 3; matrix products, arithmetic and copies ran while one was open for 8% -> 9% of each run, Pallas kernels for 0% -> 0%
where the time goes in v1:
time: 392 us; the launch traced here: 390 us
  waiting for transfers between devices  198 us (51%)
  other arithmetic  98.8 us (25%)
  local copies, waits for them, and re-layouts  53.9 us (14%)
  between operations  15.6 us (4%)
  matrix products  12.3 us (3%)
  starting transfers between devices  11.5 us (3%)
    psum x2, waiting for transfers between devices, shards(): gram = lax.psum(gram, over)  194 us
    another operation x3, other arithmetic, gradients(): return jnp.stack([grad_x, grad_y], axis=1).astype(jnp.bfloat16)  38.2 us
    another operation x7, other arithmetic, shards(): lower = jnp.linalg.cholesky(gram[:snaps - 1, :snaps - 1])  34.5 us
    another operation x4, other arithmetic, tri_solve(): return lax.linalg.triangular_solve(lower, right, left_side=True, lower=True)  20.1 us
    slice x3, local copies, waits for them, and re-layouts, padded_2(): lax.slice_in_dim(cells, cells.shape[dim] - width, cells.shape[dim], axis=...  16.4 us
    slice x1, local copies, waits for them, and re-layouts, shards(): snap[1:]  8.66 us
    unnamed x11, local copies, waits for them, and re-layouts  8.44 us
  transfers between devices with their start and end apart: 6, of which 3 were waited for; matrix products, arithmetic and copies ran while one was open for 9% of the time, Pallas kernels for 0%

profile of v1, /device:TPU:2, one launch (start us, length us, event | category | flops | bytes accessed | tf_op | source)
XLA Modules:
  0.0 390.3 jit_solution(2503583490976444099)
XLA Ops:
  7.2 3.9 %fusion.43 = (bf16[1,256,48,128]{3,2,1,0:T(8,128)(2,1)S(1)}, bf16[1,256,48,128]{3,2,1,0:T(8,128)(2,1)S(1)}) fusion(bf16[2,256,48,128]{3,2,1,0:T(8,128)(2,1)} %param.3), kind=kLoop, calls=%fused_computation.89 | loop fusion | bytes 12582912 | tf_op jit(solution)/shard_map/slice | solution.py:49
  12.5 1.8 collective-permute-start
  15.6 3.8 collective-permute-done.1
  20.1 3.6 pad_maximum_fusion.1
  23.7 11.6 %fusion.41 = (f32[256,52,2]{2,0,1:T(8,128)}, f32[256,52,2]{2,0,1:T(8,128)}) fusion(f32[256,52,128]{2,0,1:T(8,128)} %pad_maximum_fusion.1), kind=kLoop, calls=%fused_computation.87 | loop fusion | bytes 425984 | tf_op jit(solution)/shard_map/slice | solution.py:12
  35.4 4.7 %copy.16 = f32[256,52,2]{0,2,1:T(2,128)S(1)} copy(f32[256,52,2]{2,0,1:T(8,128)} %get-tuple-element.41) | data formatting | bytes 212992 | tf_op jit(solution)/shard_map/slice | solution.py:12
  40.1 3.5 collective-permute-start.2
  43.6 5.3 %copy.18 = f32[256,52,2]{0,2,1:T(2,128)} copy(f32[256,52,2]{2,0,1:T(8,128)} %get-tuple-element.42) | data formatting | bytes 212992 | tf_op jit(solution)/shard_map/slice | solution.py:11
  48.9 4.6 %collective-permute-start.3 = (f32[256,52,2]{0,2,1:T(2,128)}, f32[256,52,2]{0,2,1:T(2,128)}, u32[]{:S(2)}, u32[]{:S(2)}) collective-permute-start(f32[256,52,2]{0,2,1:T(2,128)} %copy.18), channel_id=1, source_target_pairs={{1,0},{2,1},{3,2},{4,3},{5,4},{6,5},{7,6},{8,7},{9,8},{10,9},{11,1... | collective-permute-start | bytes 319496 | tf_op jit(solution)/shard_map/ppermute | solution.py:17
  53.5 11.1 %fusion.17 = bf16[256,1,48,128]{3,0,2,1:T(8,128)(2,1)S(1)} fusion(f32[256,2,128]{2,0,1:T(8,128)} %copy-done.2, f32[256,48,128]{2,0,1:T(8,128)} %copy-done, f32[256,2,128]{2,0,1:T(8,128)S(1)} %collective-permute-done), kind=kLoop, calls=%fused_computation.36 | loop fusion | flops 17301504 | bytes 9961472 | tf_op jit(solution)/shard_map/stack | solution.py:41
  64.6 5.0 %copy.17 = f32[256,52,2]{2,0,1:T(8,128)} copy(f32[256,52,2]{0,2,1:T(2,128)} %collective-permute-done.2) | data formatting | bytes 212992 | tf_op jit(solution)/shard_map/ppermute | solution.py:15
  69.6 5.1 %copy.19 = f32[256,52,2]{2,0,1:T(8,128)} copy(f32[256,52,2]{0,2,1:T(2,128)} %collective-permute-done.3) | data formatting | bytes 212992 | tf_op jit(solution)/shard_map/ppermute | solution.py:17
  74.7 21.3 %fusion.18 = bf16[256,1,48,128]{3,0,2,1:T(8,128)(2,1)S(1)} fusion(f32[256,52,2]{2,0,1:T(8,128)} %copy.19, f32[256,2,128]{2,0,1:T(8,128)} %copy-done.2, f32[256,48,128]{2,0,1:T(8,128)} %copy-done, f32[256,2,128]{2,0,1:T(8,128)S(1)} %collective-permute-done, f32[256,52,2]{2,0,1:T(8,128)} %copy.17), kind=kLoop, calls=%fused_computation.37 | loop fusion | flops 29884416 | bytes 10174464 | tf_op jit(solution)/shard_map/stack | solution.py:41
  97.6 2.5 fusion.20
  100.5 98.4 %all-reduce.5.cloned.1.call-done = f32[256,256]{0,1:T(8,128)} async-done(((f32[256,256]{0,1:T(8,128)}), f32[256,256]{0,1:T(8,128)}) %all-reduce.5.cloned.1.call-update) | async-done | bytes 262160 | tf_op jit(solution)/shard_map/psum | solution.py:59
  199.0 5.9 %fusion.8 = bf16[255,2,48,128]{3,0,2,1:T(8,128)(2,1)} fusion(bf16[256,1,48,128]{3,0,2,1:T(8,128)(2,1)S(1)} %fusion.17, bf16[256,1,48,128]{3,0,2,1:T(8,128)(2,1)} %copy-done.1), kind=kLoop, calls=%fused_computation.17 | loop fusion | flops 3133440 | bytes 12558336 | tf_op jit(solution)/shard_map/stack | solution.py:41
  204.8 8.7 %copy.22 = bf16[255,2,48,128]{0,3,2,1:T(8,128)(2,1)} copy(bf16[255,2,48,128]{3,0,2,1:T(8,128)(2,1)} %fusion.8) | data formatting | bytes 12533760 | tf_op jit(solution)/shard_map/slice | solution.py:65
  213.5 96.0 %all-reduce.7.cloned.1.call-done = f32[256,256]{0,1:T(8,128)} async-done(((f32[256,256]{0,1:T(8,128)}), f32[256,256]{0,1:T(8,128)}) %all-reduce.7.cloned.1.call-update) | async-done | bytes 262160 | tf_op jit(solution)/shard_map/psum | solution.py:59
  311.6 11.7 %cholesky.51 = f32[128,128]{1,0:T(8,128)S(1)} custom-call(f32[128,128]{1,0:T(8,128)S(1)} %cholesky.124), custom_call_target="Cholesky" | custom-call | tf_op jit(solution)/shard_map/jit(cholesky)/cholesky | solution.py:60
  323.3 9.8 %custom-call.14 = f32[1,128,128]{1,2,0:T(8,128)S(1)} custom-call(f32[1,128,128]{2,1,0:T(8,128)S(1)} %get-tuple-element.50), custom_call_target="InvertDiagBlocksLowerTriangular" | custom-call | tf_op jit(solution)/shard_map/jit(cholesky)/cholesky | solution.py:60
  333.6 11.6 %cholesky.110 = f32[127,127]{1,0:T(8,128)S(1)} custom-call(f32[127,127]{1,0:T(8,128)S(1)} %convolution_subtract_fusion.3), custom_call_target="Cholesky" | custom-call | tf_op jit(solution)/shard_map/jit(cholesky)/cholesky | solution.py:60
  348.0 19.9 %custom-call.17 = f32[2,128,128]{1,2,0:T(8,128)S(1)} custom-call(f32[2,128,128]{2,1,0:T(8,128)S(1)} %pad_maximum_fusion.15), custom_call_target="InvertDiagBlocksLowerTriangular" | custom-call | tf_op jit(solution)/shard_map/triangular_solve/custom-call.0 | solution.py:25
  373.7 4.6 %convolution_convert_fusion = bf16[255,12288]{1,0:T(8,128)(2,1)S(1)} fusion(bf16[255,12288]{0,1:T(8,128)(2,1)} %bitcast.62, bf16[127,255]{1,0:T(8,128)(2,1)S(1)} %fusion.35, f32[128,255]{1,0:T(8,128)S(1)} %fusion.27), kind=kOutput, calls=%fused_computation | convolution fusion | flops 1601447936 | bytes 12729090 | tf_op jit(solution)/shard_map/dot_general | solution.py:65
  379.7 3.8 slice.212
  (46 shorter events, 16.5 us)
Async XLA Ops:
  7.2 191.8 %all-reduce.5.cloned.1.call-start = ((), (), s32[]{:S(2)}) async-start(), calls=%async_computation | async-start | bytes 524288 | tf_op jit(solution)/shard_map/psum | solution.py:59
  12.5 6.9 %copy-start = (f32[256,48,128]{2,0,1:T(8,128)}, f32[256,48,128]{2,0,1:T(8,128)S(1)}, u32[]{:S(2)}) copy-start(f32[256,48,128]{2,0,1:T(8,128)S(1)} %divide_bitcast_fusion) | copy-start | bytes 18874372
  12.5 3.1 collective-permute-start
  14.3 5.1 %collective-permute-start.1 = (f32[256,2,128]{2,0,1:T(8,128)S(1)}, f32[256,2,128]{2,0,1:T(8,128)S(1)}, u32[]{:S(2)}, u32[]{:S(2)}) collective-permute-start(f32[256,2,128]{2,0,1:T(8,128)S(1)} %get-tuple-element.44), channel_id=1, source_target_pairs={{16,0},{32,16},{48,32},{64,48},{80,64},{96,80},{112,96},{128,112},... | collective-permute-start | bytes 786440 | tf_op jit(solution)/shard_map/ppermute | solution.py:17
  19.4 0.7 copy-start.2
  40.1 24.5 %collective-permute-start.2 = (f32[256,52,2]{0,2,1:T(2,128)S(1)}, f32[256,52,2]{0,2,1:T(2,128)}, u32[]{:S(2)}, u32[]{:S(2)}) collective-permute-start(f32[256,52,2]{0,2,1:T(2,128)S(1)} %copy.16), channel_id=1, source_target_pairs={{0,1},{1,2},{2,3},{3,4},{4,5},{5,6},{6,7},{7,8},{8,9},{9,10},{10,1... | collective-permute-start | bytes 319496 | tf_op jit(solution)/shard_map/ppermute | solution.py:15
  48.9 20.7 %collective-permute-start.3 = (f32[256,52,2]{0,2,1:T(2,128)}, f32[256,52,2]{0,2,1:T(2,128)}, u32[]{:S(2)}, u32[]{:S(2)}) collective-permute-start(f32[256,52,2]{0,2,1:T(2,128)} %copy.18), channel_id=1, source_target_pairs={{1,0},{2,1},{3,2},{4,3},{5,4},{6,5},{7,6},{8,7},{9,8},{10,9},{11,1... | collective-permute-start | bytes 319496 | tf_op jit(solution)/shard_map/ppermute | solution.py:17
  96.0 1.7 copy-start.1
  100.2 209.3 %all-reduce.7.cloned.1.call-start = ((), (), s32[]{:S(2)}) async-start(), calls=%async_computation.1 | async-start | bytes 524288 | tf_op jit(solution)/shard_map/psum | solution.py:59
  204.8 143.1 %copy-start.3 = (f32[128,1]{1,0:T(8,128)S(1)}, f32[128,1]{1,0:T(8,128)}, u32[]{:S(2)}) copy-start(f32[128,1]{1,0:T(8,128)} %constant.87.clone.3) | copy-start | bytes 1540
Sparse Core Ops, SparseCore 0:
  100.3 98.5 all-reduce.4
  201.3 108.0 all-reduce.6
